TPU v7x, 32 devices: a whole 2x2x4 slice. The times are simulated.
32 devices in a mesh: chain: 8 (over z, x), grp: 4 (over y, core).
Axes of the slice: x: 2, y: 2, z: 4, core: 2. Of those that a mesh axis runs over, the one named last changes fastest.
Arguments:
- right_side: float32 [16, 4, 64, 128], P('chain', 'grp'), may hold values from -0.8 to 0.8
- factor: float32 [16, 4, 2, 128, 128], P('chain', 'grp'), may hold values from -1 to 1
- inverse_diag: float32 [16, 4, 128, 128], P('chain', 'grp'), as said below
- pattern: int32 [16, 4, 2], P('chain'), may hold values from 0 to 3, as said below
Outputs:
- forward_result: float32 [16, 4, 64, 128], P('chain', 'grp')
- solution: float32 [16, 4, 64, 128], P('chain', 'grp')
Inputs may be any that keep to these rules, and one draw needn't show every extreme that they name: `pattern`: the 2 entries of one supernode are different supernodes of the previous level. `inverse_diag`: every block is lower triangular with a diagonal between 0.75 and 1.05.
All inputs are finite; a program needn't handle non-finite values.
Results may differ from a plain program's by a relative error of at most 0.0002.
Values sent between devices are 32-bit elements; how exact they have to be, the bound alone decides.
No kernel may reach another device: no remote copies, remote signals or barrier semaphores. Data moves between devices by JAX's collectives and lax.ppermute only.
A program may use at most 320 MiB of HBM per device.

v0:
```python
import jax
import jax.numpy as jnp
from jax import lax
from jax.sharding import PartitionSpec as P

PRECISE = lax.Precision.HIGHEST


def carried_in(value, axis, join, neutral, backward):
    count, mine = (lax.axis_size(axis), lax.axis_index(axis))
    pieces = jax.tree.map(lambda part: lax.all_gather(part, axis), value)
    if backward:
        pieces = jax.tree.map(lambda part: part[::-1], pieces)
        mine = count - 1 - mine
    subtotal = jax.tree.map(
        lambda part, zero: jnp.full_like(part, 0) + jnp.asarray(zero, part.dtype), value, neutral
    )

    def hop(position, subtotal):
        longer = join(subtotal, jax.tree.map(lambda part: part[position], pieces))
        return jax.tree.map(lambda new, old: jnp.where(position < mine, new, old), longer, subtotal)

    return lax.fori_loop(0, count - 1, hop, subtotal)


def matmul(left_side, right_factor):
    return jnp.dot(left_side, right_factor, precision=PRECISE, preferred_element_type=jnp.float32)


def matmul_trans(left_side, right_factor):
    return lax.dot_general(
        left_side,
        right_factor,
        (((1,), (1,)), ((), ())),
        precision=PRECISE,
        preferred_element_type=jnp.float32,
    )


def combine_forward(earlier_map, later_map):
    return (
        matmul(earlier_map[0], later_map[0]),
        matmul(earlier_map[1], later_map[0]) + later_map[1],
    )


def combine_backward(earlier_map, later_map):
    return (
        matmul(later_map[0], earlier_map[0]),
        matmul_trans(earlier_map[1], later_map[0]) + later_map[1],
    )


def fold_maps(running, inputs):
    return ((matmul(running[0], inputs[0]), matmul(running[1], inputs[0]) + inputs[1]), None)


def forward_step(previous, inputs):
    updated = matmul(previous, inputs[0]) + inputs[1]
    return (updated, updated)


def back_fold(running, inputs):
    return (matmul_trans(running - inputs[1], inputs[0]), None)


def shards(right_side, factor, inverse_diag, pattern):
    levels = right_side.shape[0]
    samples = right_side.shape[2]
    sup_rows = right_side.shape[3]
    groups = lax.axis_size("grp")
    level_rows = groups * sup_rows
    my_group = lax.axis_index("grp")
    scaled = jnp.einsum(
        "lgti,lgkij->lgktj",
        inverse_diag,
        factor,
        precision=PRECISE,
        preferred_element_type=jnp.float32,
    )
    lifted = jnp.einsum(
        "lgsi,lgti->lgst",
        right_side,
        inverse_diag,
        precision=PRECISE,
        preferred_element_type=jnp.float32,
    )
    blocks, offsets = (
        lax.all_gather(scaled, "grp", axis=1, tiled=True),
        lax.all_gather(lifted, "grp", axis=1, tiled=True),
    )
    onehot = (pattern[..., None] == jnp.arange(groups, dtype=jnp.int32)).astype(jnp.float32)
    level_maps = -jnp.einsum(
        "lgkh,lgktj->lhjgt", onehot, blocks, precision=PRECISE, preferred_element_type=jnp.float32
    )
    level_maps = level_maps.reshape(levels, level_rows, level_rows)
    sources = offsets.transpose(0, 2, 1, 3).reshape(levels, samples, level_rows)
    (total_map, total_shift), _ = lax.scan(
        fold_maps, (level_maps[0], sources[0]), (level_maps[1:], sources[1:])
    )
    neutral = (
        jnp.eye(level_rows, dtype=jnp.float32),
        jnp.zeros((samples, level_rows), jnp.float32),
    )
    _, incoming = carried_in((total_map, total_shift), "chain", combine_forward, neutral, False)
    _, solved = lax.scan(forward_step, incoming, (level_maps, sources))
    forward_own = lax.dynamic_slice_in_dim(solved, my_group * sup_rows, sup_rows, 2)
    back_shift, _ = lax.scan(
        back_fold, jnp.zeros((samples, level_rows), jnp.float32), (level_maps, solved), reverse=True
    )
    _, arriving = carried_in((total_map, back_shift), "chain", combine_backward, neutral, True)
    own_inverse = inverse_diag[:, 0]

    def back_step(running, inputs):
        level_map, forward_rows, inverse = inputs
        own_rows = lax.dynamic_slice_in_dim(forward_rows, my_group * sup_rows, sup_rows, 1)
        own_pending = lax.dynamic_slice_in_dim(running, my_group * sup_rows, sup_rows, 1)
        answer = matmul(own_rows - own_pending, inverse)
        return (matmul_trans(running - forward_rows, level_map), answer)

    _, answers = lax.scan(back_step, arriving, (level_maps, solved, own_inverse), reverse=True)
    return (forward_own[:, None], answers[:, None])


def solution(mesh):
    return jax.shard_map(
        shards,
        mesh=mesh,
        in_specs=(
            P("chain", "grp", None, None),
            P("chain", "grp", None, None, None),
            P("chain", "grp", None, None),
            P("chain", None, None),
        ),
        out_specs=(P("chain", "grp", None, None), P("chain", "grp", None, None)),
        check_vma=False,
    )
```

profile of v0, /device:TPU:0, one launch (start us, length us, event | category | flops | bytes accessed | tf_op | source)
XLA Modules:
  0.0 289.6 jit_solution(16148861564298682824)
XLA Ops:
  7.2 0.9 copy-done
  8.1 1.5 convolution_bitcast_fusion.4
  9.6 0.8 copy.22
  10.5 0.8 copy.23
  11.3 1.3 fusion.50
  12.6 7.2 %all-gather.1 = f32[2,256,128]{2,1,0:T(8,128)S(1)} all-gather(f32[2,64,128]{2,1,0:T(8,128)S(1)} %fusion.50), channel_id=3, replica_groups=mesh['chain'=8,'grp'=4] {'grp'}, dimensions={1}, use_global_device_ids=true | all-gather | bytes 327680 | tf_op jit(solution)/shard_map/all_gather | solution.py:90
  20.0 0.7 fusion.58
  20.8 9.2 %all-gather.9.cloned.1.call-done = f32[2,4,2,128,128]{4,3,2,0,1:T(8,128)} async-done(((f32[2,1,2,128,128]{4,3,2,0,1:T(8,128)}), f32[2,4,2,128,128]{4,3,2,0,1:T(8,128)}) %all-gather.9.cloned.1.call-update) | async-done | bytes 1048592 | tf_op jit(solution)/shard_map/all_gather | solution.py:89
  30.1 3.9 %negate_bitcast_fusion = f32[2,4,128,4,128]{2,1,4,3,0:T(4,128)S(1)} fusion(f32[2,4,2,128,128]{4,3,2,0,1:T(8,128)} %all-gather.9.cloned.1.call-done, s32[2,4,2]{2,1,0:T(4,128)S(1)} %copy.23), kind=kOutput, calls=%fused_computation.46 | convolution fusion | flops 13107264 | bytes 3145792 | tf_op jit(solution)/shard_map/lgkh,lgktj->lhjgt/dot_general | solution.py:93
  34.0 1.1 fusion.57
  35.1 1.8 convolution_add_fusion
  37.0 5.7 %fusion.39 = f32[512,512]{1,0:T(8,128)} fusion(f32[64,8,4,128]{3,2,1,0:T(4,128)} %bitcast.155, f32[64,8,4,128]{3,2,1,0:T(4,128)S(1)} %bitcast.154), kind=kOutput, calls=%fused_computation.50 | convolution fusion | flops 1610612736 | bytes 3145728 | tf_op jit(solution)/shard_map/while/body/eval_jaxpr/dot_general | solution.py:27
  42.9 1.1 reshape.43
  44.0 1.9 reshape.42
  45.9 1.9 copy.26
  47.8 29.5 %all-gather.13.cloned.1.call-done = f32[512,512]{1,0:T(8,128)} async-done(((f32[64,512]{1,0:T(8,128)}), f32[512,512]{1,0:T(8,128)}) %all-gather.13.cloned.1.call-update) | async-done | bytes 1048592 | tf_op jit(solution)/shard_map/all_gather | solution.py:11
  77.3 125.4 %all-gather.11.cloned.1.call-done = f32[4096,512]{1,0:T(8,128)} async-done(((f32[512,512]{1,0:T(8,128)}), f32[4096,512]{1,0:T(8,128)}) %all-gather.11.cloned.1.call-update) | async-done | bytes 8388624 | tf_op jit(solution)/shard_map/all_gather | solution.py:11
  202.7 14.4 %while.79 = (s32[]{:T(128)}, f32[64,512]{1,0:T(8,128)S(1)}, s32[]{:T(128)}, f32[8,512,512]{2,1,0:T(8,128)}, f32[8,64,512]{2,1,0:T(8,128)}, /*index=5*/s32[]{:T(128)}, s32[]{:T(128)}) while((s32[]{:T(128)}, f32[64,512]{1,0:T(8,128)S(1)}, s32[]{:T(128)}, f32[8,512,512]{2,1,0:T(8,128)}, f32[8,64,512]{2,1,0:T(8,128)}, ...), condition=%wide.region_1.2_spmd.clone, body=%wide.region_0.1_spmd.clone.sunk | while | flops 201457664 | bytes 1837671 | solution.py:23
  202.7 2.0 fusion.82
  204.8 2.0 fusion.82
  206.8 2.0 fusion.82
  208.9 2.0 fusion.82
  211.0 2.0 fusion.82
  213.0 2.0 fusion.82
  215.1 2.0 fusion.82
  217.1 1.7 while.76
  217.1 0.8 bitcast_dynamic-update-slice_fusion.2
  218.0 0.8 bitcast_dynamic-update-slice_fusion.2
  218.8 2.3 while.77
  218.8 1.1 fusion.75
  220.0 1.1 fusion.75
  221.1 0.6 copy-done.1
  221.8 7.6 %rev.6 = f32[8,512,512]{2,1,0:T(8,128)} reverse(f32[8,512,512]{2,1,0:T(8,128)} %get-tuple-element.945), dimensions={0} | reverse | bytes 16777216 | tf_op jit(solution)/shard_map/rev | solution.py:13
  229.4 0.6 dynamic-slice_bitcast_fusion
  230.0 30.4 %all-gather.15.cloned.1.call-done = f32[512,512]{1,0:T(8,128)} async-done(((f32[64,512]{1,0:T(8,128)}), f32[512,512]{1,0:T(8,128)}) %all-gather.15.cloned.1.call-update) | async-done | bytes 1048592 | tf_op jit(solution)/shard_map/all_gather | solution.py:11
  260.4 2.3 rev.7
  262.7 16.8 %while.80 = (s32[]{:T(128)}, f32[64,512]{1,0:T(8,128)S(1)}, s32[]{:T(128)}, f32[8,512,512]{2,1,0:T(8,128)}, f32[8,64,512]{2,1,0:T(8,128)}, /*index=5*/s32[]{:T(128)}, s32[]{:T(128)}) while((s32[]{:T(128)}, f32[64,512]{1,0:T(8,128)S(1)}, s32[]{:T(128)}, f32[8,512,512]{2,1,0:T(8,128)}, f32[8,64,512]{2,1,0:T(8,128)}, ...), condition=%wide.region_7.8_spmd.clone, body=%wide.region_6.7_spmd.clone.sunk | while | flops 201457664 | bytes 1837671 | solution.py:23
  262.7 2.4 fusion.85
  265.2 2.4 fusion.85
  267.6 2.4 fusion.85
  270.0 2.4 fusion.85
  272.4 2.4 fusion.85
  274.8 2.4 fusion.85
  277.2 2.4 fusion.85
  279.6 2.8 while.78
  279.9 1.1 fusion.78
  281.3 1.1 fusion.78
  282.4 0.6 copy-done.5
  (45 shorter events, 1.4 us)
Async XLA Ops:
  7.2 1.0 copy-start
  7.2 22.9 %all-gather.9.cloned.1.call-start = ((), (), s32[]{:S(2)}) async-start(), calls=%async_computation | async-start | bytes 1310720 | tf_op jit(solution)/shard_map/all_gather | solution.py:89
  10.5 66.9 %all-gather.13.cloned.1.call-start = ((), (), s32[]{:S(2)}) async-start(), calls=%async_computation.2 | async-start | bytes 1179648 | tf_op jit(solution)/shard_map/all_gather | solution.py:11
  20.0 0.8 copy-start.3
  34.0 1.2 copy-start.4
  36.9 165.8 %all-gather.11.cloned.1.call-start = ((), (), s32[]{:S(2)}) async-start(), calls=%async_computation.1 | async-start | bytes 9437184 | tf_op jit(solution)/shard_map/all_gather | solution.py:11
  42.7 217.7 %all-gather.15.cloned.1.call-start = ((), (), s32[]{:S(2)}) async-start(), calls=%async_computation.3 | async-start | bytes 1179648 | tf_op jit(solution)/shard_map/all_gather | solution.py:11
  221.1 0.6 copy-start.1
  262.7 16.9 %copy-start.2 = (f32[2,1,128,128]{3,2,1,0:T(8,128)S(1)}, f32[2,1,128,128]{3,2,1,0:T(8,128)}, u32[]{:S(2)}) copy-start(f32[2,1,128,128]{3,2,1,0:T(8,128)} %param.16) | copy-start | bytes 393220
  282.4 0.6 copy-start.5
Sparse Core Ops, SparseCore 0:
  10.6 19.4 all-gather.8
  37.0 40.2 all-gather.12
  79.5 123.1 all-gather.10
  221.9 38.4 all-gather.14
where the time goes:
time: 290 us
  waiting for transfers between devices  195 us (67%)
  matrix products  51.5 us (18%)
  local copies, waits for them, and re-layouts  21.4 us (7%)
  between operations  13.9 us (5%)
  blocking collectives  7.25 us (2%)
    all_gather x3, waiting for transfers between devices, carried_in(): pieces = jax.tree.map(lambda part: lax.all_gather(part, axis), value)  185 us
    dot_general x13, matrix products, matmul(): jnp.dot(left_side, right_factor, precision=PRECISE, preferred_element_typ...  23.7 us
    dot_general x11, matrix products, matmul_trans(): lax.dot_general(left_side, right_factor, (((1,), (1,)), ((), ())), precis...  21 us
    rev x2, local copies, waits for them, and re-layouts, carried_in(): pieces = jax.tree.map(lambda part: part[::-1], pieces)  9.88 us
    all_gather x1, waiting for transfers between devices, shards(): lax.all_gather(scaled, 'grp', axis=1, tiled=True)  9.25 us
    all_gather x1, blocking collectives, shards(): lax.all_gather(lifted, 'grp', axis=1, tiled=True)  7.25 us
  transfers between devices with their start and end apart: 4, of which 4 were waited for; matrix products, arithmetic and copies ran while one was open for 8% of the time, Pallas kernels for 0%

commit v1 on v0

--- a/solution.py
+++ b/solution.py
@@ -4,6 +4,18 @@
 from jax.sharding import PartitionSpec as P
 
 PRECISE = lax.Precision.HIGHEST
+
+
+def gather_by_bits(value, axis, dim):
+    ways, here = (lax.axis_size(axis), lax.axis_index(axis))
+    grown, reach = (value, 1)
+    while reach < ways:
+        theirs = lax.ppermute(grown, axis, [(d, d ^ reach) for d in range(ways)])
+        mine_first = jnp.concatenate([grown, theirs], axis=dim)
+        theirs_first = jnp.concatenate([theirs, grown], axis=dim)
+        grown = jnp.where(here & reach == 0, mine_first, theirs_first)
+        reach = 2 * reach
+    return grown
 
 
 def carried_in(value, axis, join, neutral, backward):
@@ -87,7 +99,7 @@
     )
     blocks, offsets = (
         lax.all_gather(scaled, "grp", axis=1, tiled=True),
-        lax.all_gather(lifted, "grp", axis=1, tiled=True),
+        gather_by_bits(lifted, "grp", 1),
     )
     onehot = (pattern[..., None] == jnp.arange(groups, dtype=jnp.int32)).astype(jnp.float32)
     level_maps = -jnp.einsum(

time: 290 us -> 290 us (level)
  blocking collectives: 7.25 us -> 0 us
  starting transfers between devices: 0.34 us -> 3.82 us
  waiting for transfers between devices: 195 us -> 198 us
    all_gather x1 -> x0, blocking collectives: 7.25 us -> none  [shards(): lax.all_gather(lifted, 'grp', axis=1, tiled=True)]
    ppermute x0 -> x2, waiting for transfers between devices: none -> 3.95 us  [gather_by_bits(): theirs = lax.ppermute(grown, axis, [(d, d ^ reach) for d in range(ways)])]
    ppermute x0 -> x2, starting transfers between devices: none -> 3.48 us  [gather_by_bits(): theirs = lax.ppermute(grown, axis, [(d, d ^ reach) for d in range(ways)])]
  transfers between devices with their start and end apart: 4 -> 6, of which waited for: 4 -> 6; matrix products, arithmetic and copies ran while one was open for 8% -> 8% of each run, Pallas kernels for 0% -> 0%
where the time goes in v1:
time: 290 us
  waiting for transfers between devices  198 us (68%)
  matrix products  51.5 us (18%)
  local copies, waits for them, and re-layouts  21.3 us (7%)
  between operations  13.9 us (5%)
  starting transfers between devices  3.82 us (1%)
    all_gather x3, waiting for transfers between devices, carried_in(): pieces = jax.tree.map(lambda part: lax.all_gather(part, axis), value)  185 us
    dot_general x13, matrix products, matmul(): jnp.dot(left_side, right_factor, precision=PRECISE, preferred_element_typ...  23.7 us
    dot_general x11, matrix products, matmul_trans(): lax.dot_general(left_side, right_factor, (((1,), (1,)), ((), ())), precis...  21 us
    rev x2, local copies, waits for them, and re-layouts, carried_in(): pieces = jax.tree.map(lambda part: part[::-1], pieces)  9.88 us
    all_gather x1, waiting for transfers between devices, shards(): lax.all_gather(scaled, 'grp', axis=1, tiled=True)  8.38 us
  transfers between devices with their start and end apart: 6, of which 6 were waited for; matrix products, arithmetic and copies ran while one was open for 8% of the time, Pallas kernels for 0%

profile of v1, /device:TPU:0, one launch (start us, length us, event | category | flops | bytes accessed | tf_op | source)
XLA Modules:
  0.0 289.6 jit_solution(7165142452482208520)
XLA Ops:
  7.2 0.9 copy-done
  8.1 1.5 convolution_bitcast_fusion.4
  9.6 0.8 copy.22
  10.5 1.3 convolution_bitcast_fusion.5
  12.4 0.9 collective-permute-done
  13.3 2.9 %collective-permute-start.1 = (f32[2,2,64,128]{3,2,0,1:T(8,128)S(1)}, f32[2,2,64,128]{3,2,0,1:T(8,128)S(1)}, u32[]{:S(2)}, u32[]{:S(2)}) collective-permute-start(f32[2,2,64,128]{3,2,0,1:T(8,128)S(1)} %maximum_select_fusion.1), channel_id=1, source_target_pairs={{0,2},{1,3},{2,0},{3,1},{4,6},{5,7},{6,4},{7,5},{8,10},{9,11},{10,... | collective-permute-start | bytes 393224 | tf_op jit(solution)/shard_map/ppermute | solution.py:13
  16.2 0.8 copy.23
  17.0 3.0 %collective-permute-done.1 = f32[2,2,64,128]{3,2,0,1:T(8,128)S(1)} collective-permute-done((f32[2,2,64,128]{3,2,0,1:T(8,128)S(1)}, f32[2,2,64,128]{3,2,0,1:T(8,128)S(1)}, u32[]{:S(2)}, u32[]{:S(2)}) %collective-permute-start.1) | collective-permute-done | bytes 131104 | tf_op jit(solution)/shard_map/ppermute | solution.py:13
  20.0 0.8 fusion.47
  20.9 0.7 copy.25
  21.7 8.4 %all-gather.8.cloned.1.call-done = f32[2,4,2,128,128]{4,3,2,0,1:T(8,128)} async-done(((f32[2,1,2,128,128]{4,3,2,0,1:T(8,128)}), f32[2,4,2,128,128]{4,3,2,0,1:T(8,128)}) %all-gather.8.cloned.1.call-update) | async-done | bytes 1048592 | tf_op jit(solution)/shard_map/all_gather | solution.py:101
  30.0 3.9 %negate_bitcast_fusion = f32[2,4,128,4,128]{2,1,4,3,0:T(4,128)S(1)} fusion(f32[2,4,2,128,128]{4,3,2,0,1:T(8,128)} %all-gather.8.cloned.1.call-done, s32[2,4,2]{2,1,0:T(4,128)S(1)} %copy.23), kind=kOutput, calls=%fused_computation.46 | convolution fusion | flops 13107264 | bytes 3145792 | tf_op jit(solution)/shard_map/lgkh,lgktj->lhjgt/dot_general | solution.py:105
  34.0 1.2 fusion.58
  35.1 1.8 convolution_add_fusion
  37.0 5.7 %fusion.39 = f32[512,512]{1,0:T(8,128)} fusion(f32[64,8,4,128]{3,2,1,0:T(4,128)} %bitcast.160, f32[64,8,4,128]{3,2,1,0:T(4,128)S(1)} %bitcast.159), kind=kOutput, calls=%fused_computation.51 | convolution fusion | flops 1610612736 | bytes 3145728 | tf_op jit(solution)/shard_map/while/body/eval_jaxpr/dot_general | solution.py:39
  43.0 1.0 copy.59
  43.9 1.9 reshape.42
  45.8 1.9 copy.28
  47.7 29.6 %all-gather.12.cloned.1.call-done = f32[512,512]{1,0:T(8,128)} async-done(((f32[64,512]{1,0:T(8,128)}), f32[512,512]{1,0:T(8,128)}) %all-gather.12.cloned.1.call-update) | async-done | bytes 1048592 | tf_op jit(solution)/shard_map/all_gather | solution.py:23
  77.4 125.4 %all-gather.10.cloned.1.call-done = f32[4096,512]{1,0:T(8,128)} async-done(((f32[512,512]{1,0:T(8,128)}), f32[4096,512]{1,0:T(8,128)}) %all-gather.10.cloned.1.call-update) | async-done | bytes 8388624 | tf_op jit(solution)/shard_map/all_gather | solution.py:23
  202.7 14.4 %while.79 = (s32[]{:T(128)}, f32[64,512]{1,0:T(8,128)S(1)}, s32[]{:T(128)}, f32[8,512,512]{2,1,0:T(8,128)}, f32[8,64,512]{2,1,0:T(8,128)}, /*index=5*/s32[]{:T(128)}, s32[]{:T(128)}) while((s32[]{:T(128)}, f32[64,512]{1,0:T(8,128)S(1)}, s32[]{:T(128)}, f32[8,512,512]{2,1,0:T(8,128)}, f32[8,64,512]{2,1,0:T(8,128)}, ...), condition=%wide.region_1.2_spmd.clone, body=%wide.region_0.1_spmd.clone.sunk | while | flops 201457664 | bytes 1837671 | solution.py:35
  202.7 2.0 fusion.83
  204.8 2.0 fusion.83
  206.9 2.0 fusion.83
  208.9 2.0 fusion.83
  211.0 2.0 fusion.83
  213.0 2.0 fusion.83
  215.1 2.0 fusion.83
  217.1 1.7 while.76
  217.2 0.8 bitcast_dynamic-update-slice_fusion.2
  218.0 0.8 bitcast_dynamic-update-slice_fusion.2
  218.8 2.3 while.77
  218.9 1.1 fusion.76
  220.0 1.1 fusion.76
  221.8 7.6 %rev.6 = f32[8,512,512]{2,1,0:T(8,128)} reverse(f32[8,512,512]{2,1,0:T(8,128)} %get-tuple-element.947), dimensions={0} | reverse | bytes 16777216 | tf_op jit(solution)/shard_map/rev | solution.py:25
  230.0 30.4 %all-gather.14.cloned.1.call-done = f32[512,512]{1,0:T(8,128)} async-done(((f32[64,512]{1,0:T(8,128)}), f32[512,512]{1,0:T(8,128)}) %all-gather.14.cloned.1.call-update) | async-done | bytes 1048592 | tf_op jit(solution)/shard_map/all_gather | solution.py:23
  260.4 2.3 rev.7
  262.7 16.8 %while.80 = (s32[]{:T(128)}, f32[64,512]{1,0:T(8,128)S(1)}, s32[]{:T(128)}, f32[8,512,512]{2,1,0:T(8,128)}, f32[8,64,512]{2,1,0:T(8,128)}, /*index=5*/s32[]{:T(128)}, s32[]{:T(128)}) while((s32[]{:T(128)}, f32[64,512]{1,0:T(8,128)S(1)}, s32[]{:T(128)}, f32[8,512,512]{2,1,0:T(8,128)}, f32[8,64,512]{2,1,0:T(8,128)}, ...), condition=%wide.region_7.8_spmd.clone, body=%wide.region_6.7_spmd.clone.sunk | while | flops 201457664 | bytes 1837671 | solution.py:35
  262.7 2.4 fusion.86
  265.2 2.4 fusion.86
  267.6 2.4 fusion.86
  270.0 2.4 fusion.86
  272.4 2.4 fusion.86
  274.8 2.4 fusion.86
  277.2 2.4 fusion.86
  279.6 2.8 while.78
  279.9 1.1 fusion.79
  281.3 1.1 fusion.79
  (49 shorter events, 3.7 us)
Async XLA Ops:
  7.2 1.0 copy-start
  7.2 22.9 %all-gather.8.cloned.1.call-start = ((), (), s32[]{:S(2)}) async-start(), calls=%async_computation | async-start | bytes 1310720 | tf_op jit(solution)/shard_map/all_gather | solution.py:101
  10.5 66.9 %all-gather.12.cloned.1.call-start = ((), (), s32[]{:S(2)}) async-start(), calls=%async_computation.2 | async-start | bytes 1179648 | tf_op jit(solution)/shard_map/all_gather | solution.py:23
  11.8 1.5 collective-permute-start
  13.3 6.7 %collective-permute-start.1 = (f32[2,2,64,128]{3,2,0,1:T(8,128)S(1)}, f32[2,2,64,128]{3,2,0,1:T(8,128)S(1)}, u32[]{:S(2)}, u32[]{:S(2)}) collective-permute-start(f32[2,2,64,128]{3,2,0,1:T(8,128)S(1)} %maximum_select_fusion.1), channel_id=1, source_target_pairs={{0,2},{1,3},{2,0},{3,1},{4,6},{5,7},{6,4},{7,5},{8,10},{9,11},{10,... | collective-permute-start | bytes 393224 | tf_op jit(solution)/shard_map/ppermute | solution.py:13
  34.0 1.2 copy-start.3
  36.9 165.8 %all-gather.10.cloned.1.call-start = ((), (), s32[]{:S(2)}) async-start(), calls=%async_computation.1 | async-start | bytes 9437184 | tf_op jit(solution)/shard_map/all_gather | solution.py:23
  42.7 217.7 %all-gather.14.cloned.1.call-start = ((), (), s32[]{:S(2)}) async-start(), calls=%async_computation.3 | async-start | bytes 1179648 | tf_op jit(solution)/shard_map/all_gather | solution.py:23
  221.1 0.7 copy-start.1
  262.7 16.9 %copy-start.2 = (f32[2,1,128,128]{3,2,1,0:T(8,128)S(1)}, f32[2,1,128,128]{3,2,1,0:T(8,128)}, u32[]{:S(2)}) copy-start(f32[2,1,128,128]{3,2,1,0:T(8,128)} %param.16) | copy-start | bytes 393220
  282.4 0.6 copy-start.4
Sparse Core Ops, SparseCore 0:
  10.6 19.4 all-gather.7
  37.1 40.2 all-gather.11
  79.5 123.1 all-gather.9
  221.9 38.4 all-gather.13
